TPU v7x, 512 devices: a whole 4x4x16 slice. The times are simulated.
512 devices in a mesh: gx: 64 (over z, y), gy: 8 (over x, core).
Axes of the slice: x: 4, y: 4, z: 16, core: 2. Of those that a mesh axis runs over, the one named last changes fastest.
Arguments:
- rhs: float32 [64, 8, 128, 128], P('gx', 'gy'), may hold values from -57 to 57
- face_rows: int32 [64, 8, 4, 128], P('gx', 'gy'), may hold values from 0 to 127
- margin_weight: float32 [64, 8, 4, 128], P('gx', 'gy'), may hold values from 0.2 to 1
- local_blocks: bfloat16 [64, 8, 1, 128, 128], P('gx', 'gy'), may hold values from -0.4 to 4.4
- subdomain_inverse: bfloat16 [64, 8, 128, 640], P('gx', 'gy'), may hold values from -0.4 to 1.8
- coarse_basis: bfloat16 [64, 8, 128, 32], P('gx', 'gy'), may hold values from -0.5 to 0.5
- coarse_inverse: bfloat16 [64, 8, 32, 16384], P('gx', 'gy'), may hold values from -0.09765625 to 0.09765625
- coarse_map: int32 [512], replicated, may hold values from 0 to 511, each once
Outputs:
- solution: float32 [64, 8, 128, 128], P('gx', 'gy')
- relative_residual: float32 [128], replicated
Inputs may be any that keep to these rules, and one draw needn't show every extreme that they name: `face_rows`: rows of the subdomain, repeats possible. `coarse_map`: every position once.
All inputs are finite; a program needn't handle non-finite values.
Results may differ from a plain program's by a relative error of at most 0.004.
Values may be sent and summed in bfloat16 or wider, within the bound.
No kernel may reach another device: no remote copies, remote signals or barrier semaphores. Data moves between devices by JAX's collectives and lax.ppermute only.
A program may use at most 64 MiB of HBM per device.

v0:
```python
import jax
import jax.numpy as jnp
from jax import lax
from jax.sharding import PartitionSpec as P

EPSILON = 1e-06


def padded(shard, sides, width):
    for axis, dim in sides:
        count, length = (lax.axis_size(axis), shard.shape[dim])
        up = [(i, (i + 1) % count) for i in range(count - 1)]
        down = [(j, i) for i, j in up]
        last = lax.slice_in_dim(shard, length - width, length, axis=dim)
        initial = lax.slice_in_dim(shard, 0, width, axis=dim)
        before = lax.ppermute(last, axis, up)
        after = lax.ppermute(initial, axis, down)
        shard = jnp.concatenate([before, shard, after], axis=dim)
    return shard


def least_squares(scale_norm, first_dot, first_norm, cross_dot, second_dot, second_norm):
    radius_one = jnp.sqrt(first_dot * first_dot + first_norm * first_norm)
    cosine_one = first_dot / radius_one
    sine_one = first_norm / radius_one
    upper_entry = cosine_one * cross_dot + sine_one * second_dot
    lower_entry = cosine_one * second_dot - sine_one * cross_dot
    radius_two = jnp.sqrt(lower_entry * lower_entry + second_norm * second_norm)
    cosine_two = lower_entry / radius_two
    sine_two = second_norm / radius_two
    weight_two = -cosine_two * sine_one * scale_norm / radius_two
    weight_one = (cosine_one * scale_norm - upper_entry * weight_two) / radius_one
    return (weight_one, weight_two, sine_one * sine_two)


def on_device(
    rhs,
    face_rows,
    margin_weight,
    local_blocks,
    subdomain_inverse,
    coarse_basis,
    coarse_inverse,
    coarse_map,
):
    right_side = rhs[0, 0]
    margin_rows = face_rows[0, 0]
    margin_weights = margin_weight[0, 0]
    local_block = local_blocks[0, 0]
    inverse_rows = subdomain_inverse[0, 0]
    basis = coarse_basis[0, 0]
    coarse_rows = coarse_inverse[0, 0]
    owned_rows = right_side.shape[0]
    system_count = right_side.shape[1]
    basis_count = basis.shape[1]
    block_rows = local_block.shape[1]
    positions = (
        coarse_map[:, None] * basis_count + jnp.arange(basis_count, dtype=jnp.int32)[None, :]
    ).reshape(-1)
    permuted = jnp.take(coarse_rows, positions, axis=1)

    def neighbour_margin(rounded):
        face_packs = rounded[margin_rows]
        along_first = padded(face_packs[0:2], (("gx", 0),), 1)
        along_second = padded(face_packs[2:4], (("gy", 0),), 1)
        return jnp.stack([along_first[0], along_first[3], along_second[0], along_second[3]], axis=0)

    def add_piece(shard_rows):
        return jnp.dot(permuted, shard_rows, preferred_element_type=jnp.float32)

    def precondition(vector):
        rounded = vector.astype(jnp.bfloat16)
        extended = jnp.concatenate(
            [rounded, neighbour_margin(rounded).reshape(-1, system_count)], axis=0
        )
        local_part = jnp.dot(inverse_rows, extended, preferred_element_type=jnp.float32)
        residual = lax.dot_general(
            basis, rounded, (((0,), (0,)), ((), ())), preferred_element_type=jnp.float32
        ).astype(jnp.bfloat16)
        solved = add_piece(lax.all_gather(residual, ("gx", "gy"), axis=0, tiled=True))
        return local_part + jnp.dot(
            basis, solved.astype(jnp.bfloat16), preferred_element_type=jnp.float32
        )

    def apply_operator(vector):
        rounded = vector.astype(jnp.bfloat16)
        own_part = jnp.einsum(
            "brc,bcn->brn",
            local_block,
            rounded.reshape(-1, block_rows, system_count),
            preferred_element_type=jnp.float32,
        ).reshape(owned_rows, system_count)
        weighted = margin_weights[:, :, None] * neighbour_margin(rounded).astype(jnp.float32)
        coupling = (
            jnp.zeros((owned_rows, system_count), jnp.float32)
            .at[margin_rows.reshape(-1)]
            .add(weighted.reshape(-1, system_count))
        )
        return own_part - coupling

    def column_norm(vector):
        squares = lax.psum(jnp.sum(vector * vector, axis=0), ("gx", "gy"))
        return jnp.sqrt(squares + EPSILON)

    def project_single(vector, direction):
        return lax.psum(jnp.sum(vector * direction, axis=0), ("gx", "gy"))

    scale_norm = column_norm(right_side)
    krylov_one = right_side / scale_norm
    precond_one = precondition(krylov_one)
    applied = apply_operator(precond_one)
    first_dot = project_single(applied, krylov_one)
    remainder = applied - first_dot * krylov_one
    first_norm = column_norm(remainder)
    krylov_two = remainder / first_norm
    precond_two = precondition(krylov_two)
    applied = apply_operator(precond_two)
    cross_dot = project_single(applied, krylov_one)
    remainder = applied - cross_dot * krylov_one
    second_dot = project_single(remainder, krylov_two)
    remainder = remainder - second_dot * krylov_two
    second_norm = column_norm(remainder)
    weight_one, weight_two, relative = least_squares(
        scale_norm, first_dot, first_norm, cross_dot, second_dot, second_norm
    )
    solution = weight_one * precond_one + weight_two * precond_two
    return (solution[None, None], relative)


def solution(mesh):
    return jax.shard_map(
        on_device,
        mesh=mesh,
        in_specs=(
            P("gx", "gy", None, None),
            P("gx", "gy", None, None),
            P("gx", "gy", None, None),
            P("gx", "gy", None, None, None),
            P("gx", "gy", None, None),
            P("gx", "gy", None, None),
            P("gx", "gy", None, None),
            P(),
        ),
        out_specs=(P("gx", "gy", None, None), P()),
        check_vma=False,
    )
```

profile of v0, /device:TPU:1, one launch (start us, length us, event | category | flops | bytes accessed | tf_op | source)
XLA Modules:
  0.0 1066.4 jit_solution(7111828778543676201)
XLA Ops:
  8.1 111.0 %psum.42 = f32[128]{0:T(128)S(1)} all-reduce(f32[128]{0:T(128)S(1)} %fusion.22), channel_id=1, replica_groups=mesh['gx'=64,'gy'=8] {'gx','gy'}, use_global_device_ids=true, to_apply=%region_1.2 | all-reduce | flops 128 | bytes 1024 | tf_op jit(solution)/shard_map/psum | solution.py:102
  119.1 1.6 fusion.6
  125.0 3.3 collective-permute-start.2
  129.6 1.9 collective-permute-start.3
  132.8 4.6 copy.18
  137.4 57.6 %gather_fusion.1 = bf16[16384,32]{1,0:T(8,128)(2,1)} fusion(bf16[32,16384]{0,1:T(8,128)(2,1)} %bitcast.121, s32[16384]{0:T(1024)S(1)} %broadcast_clamp_fusion), kind=kCustom, calls=%fused_computation.1 | custom fusion | bytes 2162688 | tf_op jit(solution)/shard_map/jit(_take)/gather | solution.py:60
  195.4 117.2 %all-gather.3.cloned.1.call-done = bf16[16384,128]{1,0:T(8,128)(2,1)} async-done(((bf16[32,128]{1,0:T(8,128)(2,1)}), bf16[16384,128]{1,0:T(8,128)(2,1)}) %all-gather.3.cloned.1.call-update) | async-done | bytes 4194320 | tf_op jit(solution)/shard_map/all_gather | solution.py:80
  312.7 7.1 convolution_add_fusion.1
  319.9 1.3 gather_fusion.2
  321.2 3.4 collective-permute-start.4
  324.6 3.6 collective-permute-start.6
  329.5 1.9 collective-permute-start.7
  331.5 1.4 collective-permute-done.5
  332.9 1.9 collective-permute-done.7
  334.8 2.4 scatter_custom_fusion
  337.4 102.7 %psum.43 = f32[128]{0:T(128)S(1)} all-reduce(f32[128]{0:T(128)S(1)} %get-tuple-element.29), channel_id=1, replica_groups=mesh['gx'=64,'gy'=8] {'gx','gy'}, use_global_device_ids=true, to_apply=%region_4.5 | all-reduce | flops 128 | bytes 1024 | tf_op jit(solution)/shard_map/psum | solution.py:106
  440.2 98.7 %psum.44 = f32[128]{0:T(128)S(1)} all-reduce(f32[128]{0:T(128)S(1)} %multiply_reduce_fusion.3), channel_id=1, replica_groups=mesh['gx'=64,'gy'=8] {'gx','gy'}, use_global_device_ids=true, to_apply=%region_6.7 | all-reduce | flops 128 | bytes 1024 | tf_op jit(solution)/shard_map/psum | solution.py:102
  541.1 2.4 collective-permute-start.8
  543.4 1.9 collective-permute-start.10
  546.7 2.6 collective-permute-start.11
  552.2 180.1 %all-gather.5.cloned.1.call-done = bf16[16384,128]{1,0:T(8,128)(2,1)} async-done(((bf16[32,128]{1,0:T(8,128)(2,1)}), bf16[16384,128]{1,0:T(8,128)(2,1)}) %all-gather.5.cloned.1.call-update) | async-done | bytes 4194320 | tf_op jit(solution)/shard_map/all_gather | solution.py:80
  732.2 7.1 convolution_add_fusion
  739.4 1.3 gather_fusion.4
  740.8 3.4 collective-permute-start.12
  744.2 3.6 collective-permute-start.14
  749.1 1.9 collective-permute-start.15
  751.1 1.4 collective-permute-done.13
  752.5 1.9 collective-permute-done.15
  754.4 2.4 scatter_custom_fusion.1
  757.0 102.7 %psum.45 = f32[128]{0:T(128)S(1)} all-reduce(f32[128]{0:T(128)S(1)} %get-tuple-element.31), channel_id=1, replica_groups=mesh['gx'=64,'gy'=8] {'gx','gy'}, use_global_device_ids=true, to_apply=%region_9.10 | all-reduce | flops 128 | bytes 1024 | tf_op jit(solution)/shard_map/psum | solution.py:106
  859.8 98.7 %psum.46 = f32[128]{0:T(128)S(1)} all-reduce(f32[128]{0:T(128)S(1)} %multiply_reduce_fusion.1), channel_id=1, replica_groups=mesh['gx'=64,'gy'=8] {'gx','gy'}, use_global_device_ids=true, to_apply=%region_11.12 | all-reduce | flops 128 | bytes 1024 | tf_op jit(solution)/shard_map/psum | solution.py:106
  958.5 99.6 %psum.47 = f32[128]{0:T(128)S(1)} all-reduce(f32[128]{0:T(128)S(1)} %multiply_reduce_fusion), channel_id=1, replica_groups=mesh['gx'=64,'gy'=8] {'gx','gy'}, use_global_device_ids=true, to_apply=%region_13.14 | all-reduce | flops 128 | bytes 1024 | tf_op jit(solution)/shard_map/psum | solution.py:102
  (74 shorter events, 19.1 us)
Async XLA Ops:
  7.2 187.9 %copy-start = (bf16[1,1,128,640]{3,2,1,0:T(8,128)(2,1)S(1)}, bf16[1,1,128,640]{3,2,1,0:T(8,128)(2,1)}, u32[]{:S(2)}) copy-start(bf16[1,1,128,640]{3,2,1,0:T(8,128)(2,1)} %param.12) | copy-start | bytes 491524
  7.2 305.5 %all-gather.3.cloned.1.call-start = ((), (), s32[]{:S(2)}) async-start(), calls=%async_computation | async-start | bytes 4202496 | tf_op jit(solution)/shard_map/all_gather | solution.py:80
  120.8 611.5 %all-gather.5.cloned.1.call-start = ((), (), s32[]{:S(2)}) async-start(), calls=%async_computation.1 | async-start | bytes 4202496 | tf_op jit(solution)/shard_map/all_gather | solution.py:80
  123.7 71.3 %collective-permute-start = (bf16[1,128,128]{2,1,0:T(8,128)(2,1)S(1)}, bf16[1,128,128]{2,1,0:T(8,128)(2,1)S(1)}, u32[]{:S(2)}, u32[]{:S(2)}) collective-permute-start(bf16[1,128,128]{2,1,0:T(8,128)(2,1)S(1)} %get-tuple-element.25), channel_id=1, source_target_pairs={{0,8},{8,16},{16,24},{24,32},{32,40},{40,48},{48,56},{56,64},{64,7... | collective-permute-start | bytes 98312 | tf_op jit(solution)/shard_map/ppermute | solution.py:16
  125.0 70.0 %collective-permute-start.2 = (bf16[1,128,128]{2,1,0:T(8,128)(2,1)S(1)}, bf16[1,128,128]{2,1,0:T(8,128)(2,1)S(1)}, u32[]{:S(2)}, u32[]{:S(2)}) collective-permute-start(bf16[1,128,128]{2,1,0:T(8,128)(2,1)S(1)} %get-tuple-element.26), channel_id=1, source_target_pairs={{0,1},{1,2},{2,3},{3,4},{4,5},{5,6},{6,7},{8,9},{9,10},{10,11},{11... | collective-permute-start | bytes 98312 | tf_op jit(solution)/shard_map/ppermute | solution.py:16
  128.3 66.7 %collective-permute-start.1 = (bf16[1,128,128]{2,1,0:T(8,128)(2,1)S(1)}, bf16[1,128,128]{2,1,0:T(8,128)(2,1)S(1)}, u32[]{:S(2)}, u32[]{:S(2)}) collective-permute-start(bf16[1,128,128]{2,1,0:T(8,128)(2,1)S(1)} %get-tuple-element.27), channel_id=1, source_target_pairs={{8,0},{16,8},{24,16},{32,24},{40,32},{48,40},{56,48},{64,56},{72,6... | collective-permute-start | bytes 98312 | tf_op jit(solution)/shard_map/ppermute | solution.py:17
  129.6 65.4 %collective-permute-start.3 = (bf16[1,128,128]{2,1,0:T(8,128)(2,1)S(1)}, bf16[1,128,128]{2,1,0:T(8,128)(2,1)S(1)}, u32[]{:S(2)}, u32[]{:S(2)}) collective-permute-start(bf16[1,128,128]{2,1,0:T(8,128)(2,1)S(1)} %get-tuple-element.28), channel_id=1, source_target_pairs={{1,0},{2,1},{3,2},{4,3},{5,4},{6,5},{7,6},{9,8},{10,9},{11,10},{12... | collective-permute-start | bytes 98312 | tf_op jit(solution)/shard_map/ppermute | solution.py:17
  137.4 175.2 %copy-start.5 = (bf16[1,1,128,32]{2,3,1,0:T(8,128)(2,1)S(1)}, bf16[1,1,128,32]{2,3,1,0:T(8,128)(2,1)}, u32[]{:S(2)}) copy-start(bf16[1,1,128,32]{2,3,1,0:T(8,128)(2,1)} %param.13) | copy-start | bytes 24580
  195.4 136.1 %copy-start.4 = (s32[1,1,4,128]{3,2,1,0:T(4,128)S(1)}, s32[1,1,4,128]{3,2,1,0:T(4,128)}, u32[]{:S(2)}) copy-start(s32[1,1,4,128]{3,2,1,0:T(4,128)} %param.9) | copy-start | bytes 6148
  195.4 139.4 %copy-start.3 = (f32[1,1,4,128]{3,2,1,0:T(4,128)S(1)}, f32[1,1,4,128]{3,2,1,0:T(4,128)}, u32[]{:S(2)}) copy-start(f32[1,1,4,128]{3,2,1,0:T(4,128)} %param.10) | copy-start | bytes 6148
  195.4 141.8 %copy-start.1 = (f32[1,1,128,128]{3,2,1,0:T(8,128)S(1)}, f32[1,1,128,128]{3,2,1,0:T(8,128)}, u32[]{:S(2)}) copy-start(f32[1,1,128,128]{3,2,1,0:T(8,128)} %param.8) | copy-start | bytes 196612
  195.4 141.8 %copy-start.2 = (bf16[1,1,1,128,128]{4,3,2,1,0:T(8,128)(2,1)S(1)}, bf16[1,1,1,128,128]{4,3,2,1,0:T(8,128)(2,1)}, u32[]{:S(2)}) copy-start(bf16[1,1,1,128,128]{4,3,2,1,0:T(8,128)(2,1)} %param.11) | copy-start | bytes 98308
  321.2 10.3 collective-permute-start.4
  324.6 6.9 collective-permute-start.6
  328.2 4.7 collective-permute-start.5
  329.5 5.2 collective-permute-start.7
  541.1 8.2 collective-permute-start.8
  543.4 5.8 collective-permute-start.10
  545.4 5.2 collective-permute-start.9
  546.7 5.2 collective-permute-start.11
  740.8 10.2 collective-permute-start.12
  744.2 6.8 collective-permute-start.14
  747.8 4.7 collective-permute-start.13
  749.1 5.2 collective-permute-start.15
Sparse Core Ops, SparseCore 0:
  120.9 191.7 all-gather.2
  539.8 192.3 all-gather.4
where the time goes:
time: 1070 us
  blocking collectives  614 us (57%)
  waiting for transfers between devices  307 us (29%)
  local copies, waits for them, and re-layouts  68.9 us (6%)
  starting transfers between devices  36.5 us (3%)
  matrix products  17.3 us (2%)
  between operations  14.5 us (1%)
    psum x3, blocking collectives, column_norm(): squares = lax.psum(jnp.sum(vector * vector, axis=0), ('gx', 'gy'))  309 us
    psum x3, blocking collectives, project_single(): return lax.psum(jnp.sum(vector * direction, axis=0), ('gx', 'gy'))  304 us
    all_gather x2, waiting for transfers between devices, precondition(): lax.all_gather(residual, ('gx', 'gy'), axis=0, tiled=True)  297 us
    gather x1, local copies, waits for them, and re-layouts, on_device(): permuted = jnp.take(coarse_rows, positions, axis=1)  57.6 us
    ppermute x8, starting transfers between devices, padded(): before = lax.ppermute(last, axis, up)  22.9 us
  transfers between devices with their start and end apart: 18, of which 8 were waited for; matrix products, arithmetic and copies ran while one was open for 6% of the time, Pallas kernels for 0%

commit v1 on v0

--- a/solution.py
+++ b/solution.py
@@ -77,7 +77,17 @@
         residual = lax.dot_general(
             basis, rounded, (((0,), (0,)), ((), ())), preferred_element_type=jnp.float32
         ).astype(jnp.bfloat16)
-        solved = add_piece(lax.all_gather(residual, ("gx", "gy"), axis=0, tiled=True))
+
+        def write_the_surface(block_in):
+            tile_out = lax.all_to_all(
+                jnp.stack([block_in for _ in range(lax.axis_size(("gx", "gy")))], axis=0),
+                ("gx", "gy"),
+                0,
+                0,
+            )
+            return jnp.concatenate(tile_out, 0)
+
+        solved = add_piece(write_the_surface(residual))
         return local_part + jnp.dot(
             basis, solved.astype(jnp.bfloat16), preferred_element_type=jnp.float32
         )

time: 1070 us -> 1080 us (level)
  starting transfers between devices: 36.5 us -> 68 us
  between operations: 14.5 us -> 1.17 us
    all_gather x2 -> x0, waiting for transfers between devices: 297 us -> none  [precondition(): lax.all_gather(residual, ('gx', 'gy'), axis=0, tiled=True)]
    all_to_all x0 -> x2, waiting for transfers between devices: none -> 286 us  [write_the_surface(): lax.all_to_all(jnp.stack([block_in for _ in range(lax.axis_size(('gx', 'g...]
    all_to_all x0 -> x2, starting transfers between devices: none -> 27.4 us  [write_the_surface(): lax.all_to_all(jnp.stack([block_in for _ in range(lax.axis_size(('gx', 'g...]
where the time goes in v1:
time: 1080 us; the launch traced here: 1070 us
  blocking collectives  613 us (57%)
  waiting for transfers between devices  297 us (28%)
  local copies, waits for them, and re-layouts  72.5 us (7%)
  starting transfers between devices  68 us (6%)
  matrix products  16.1 us (1%)
    psum x3, blocking collectives, column_norm(): squares = lax.psum(jnp.sum(vector * vector, axis=0), ('gx', 'gy'))  309 us
    psum x3, blocking collectives, project_single(): return lax.psum(jnp.sum(vector * direction, axis=0), ('gx', 'gy'))  304 us
    all_to_all x2, waiting for transfers between devices, write_the_surface(): lax.all_to_all(jnp.stack([block_in for _ in range(lax.axis_size(('gx', 'g...  286 us
    gather x1, local copies, waits for them, and re-layouts, on_device(): permuted = jnp.take(coarse_rows, positions, axis=1)  57.6 us
    ppermute x8, starting transfers between devices, padded(): before = lax.ppermute(last, axis, up)  27.7 us
    all_to_all x2, starting transfers between devices, write_the_surface(): lax.all_to_all(jnp.stack([block_in for _ in range(lax.axis_size(('gx', 'g...  27.4 us
  transfers between devices with their start and end apart: 18, of which 8 were waited for; matrix products, arithmetic and copies ran while one was open for 6% of the time, Pallas kernels for 0%

profile of v1, /device:TPU:1, one launch (start us, length us, event | category | flops | bytes accessed | tf_op | source)
XLA Modules:
  0.0 1074.9 jit_solution(7648320048224804574)
XLA Ops:
  1.6 111.0 %psum.42 = f32[128]{0:T(128)S(1)} all-reduce(f32[128]{0:T(128)S(1)} %fusion.22), channel_id=1, replica_groups=mesh['gx'=64,'gy'=8] {'gx','gy'}, use_global_device_ids=true, to_apply=%region_1.2 | all-reduce | flops 128 | bytes 1024 | tf_op jit(solution)/shard_map/psum | solution.py:112
  113.6 2.5 stack.13
  116.1 14.2 %all-to-all-start = ((bf16[512,32,128]{2,1,0:T(8,128)(2,1)}), bf16[512,32,128]{2,1,0:T(8,128)(2,1)}, u32[]{:S(2)}, u32[]{:S(2)}) async-start(bf16[512,32,128]{2,1,0:T(8,128)(2,1)} %stack.13), calls=%async_computation | async-start | bytes 8388608 | tf_op jit(solution)/shard_map/all_to_all | solution.py:82
  131.7 3.3 collective-permute-start
  135.0 3.7 collective-permute-start.2
  139.9 2.0 collective-permute-start.3
  142.5 3.2 copy.14
  145.7 57.6 %gather_fusion.1 = bf16[16384,32]{1,0:T(8,128)(2,1)} fusion(bf16[32,16384]{0,1:T(8,128)(2,1)} %bitcast.123, s32[16384]{0:T(1024)S(1)} %broadcast_clamp_fusion), kind=kCustom, calls=%fused_computation.1 | custom fusion | bytes 2162688 | tf_op jit(solution)/shard_map/jit(_take)/gather | solution.py:60
  203.6 114.5 %all-to-all-done = bf16[512,32,128]{2,1,0:T(8,128)(2,1)} async-done(((bf16[512,32,128]{2,1,0:T(8,128)(2,1)}), bf16[512,32,128]{2,1,0:T(8,128)(2,1)}, u32[]{:S(2)}, u32[]{:S(2)}) %all-to-all-start) | async-done | bytes 4194336 | tf_op jit(solution)/shard_map/all_to_all | solution.py:82
  318.0 7.1 convolution_add_fusion.1
  326.6 3.2 collective-permute-start.4
  329.8 3.8 collective-permute-start.6
  336.8 2.0 collective-permute-done.5
  340.2 2.4 scatter_custom_fusion
  342.7 103.0 %psum.43 = f32[128]{0:T(128)S(1)} all-reduce(f32[128]{0:T(128)S(1)} %get-tuple-element.27), channel_id=1, replica_groups=mesh['gx'=64,'gy'=8] {'gx','gy'}, use_global_device_ids=true, to_apply=%region_4.5 | all-reduce | flops 128 | bytes 1024 | tf_op jit(solution)/shard_map/psum | solution.py:116
  445.8 98.4 %psum.44 = f32[128]{0:T(128)S(1)} all-reduce(f32[128]{0:T(128)S(1)} %multiply_reduce_fusion.3), channel_id=1, replica_groups=mesh['gx'=64,'gy'=8] {'gx','gy'}, use_global_device_ids=true, to_apply=%region_6.7 | all-reduce | flops 128 | bytes 1024 | tf_op jit(solution)/shard_map/psum | solution.py:112
  544.3 2.5 stack.16
  546.8 13.2 %all-to-all-start.1 = ((bf16[512,32,128]{2,1,0:T(8,128)(2,1)}), bf16[512,32,128]{2,1,0:T(8,128)(2,1)}, u32[]{:S(2)}, u32[]{:S(2)}) async-start(bf16[512,32,128]{2,1,0:T(8,128)(2,1)} %stack.16), calls=%async_computation.1 | async-start | bytes 8388608 | tf_op jit(solution)/shard_map/all_to_all | solution.py:82
  561.4 3.3 collective-permute-start.8
  564.7 3.7 collective-permute-start.10
  569.6 2.0 collective-permute-start.11
  571.6 2.0 collective-permute-done.9
  573.6 2.0 collective-permute-done.11
  575.8 172.0 %all-to-all-done.1 = bf16[512,32,128]{2,1,0:T(8,128)(2,1)} async-done(((bf16[512,32,128]{2,1,0:T(8,128)(2,1)}), bf16[512,32,128]{2,1,0:T(8,128)(2,1)}, u32[]{:S(2)}, u32[]{:S(2)}) %all-to-all-start.1) | async-done | bytes 4194336 | tf_op jit(solution)/shard_map/all_to_all | solution.py:82
  747.8 7.1 convolution_add_fusion
  756.4 3.2 collective-permute-start.12
  759.6 3.8 collective-permute-start.14
  766.6 2.0 collective-permute-done.13
  769.9 2.4 scatter_custom_fusion.1
  772.5 102.8 %psum.45 = f32[128]{0:T(128)S(1)} all-reduce(f32[128]{0:T(128)S(1)} %get-tuple-element.29), channel_id=1, replica_groups=mesh['gx'=64,'gy'=8] {'gx','gy'}, use_global_device_ids=true, to_apply=%region_9.10 | all-reduce | flops 128 | bytes 1024 | tf_op jit(solution)/shard_map/psum | solution.py:116
  875.3 98.4 %psum.46 = f32[128]{0:T(128)S(1)} all-reduce(f32[128]{0:T(128)S(1)} %multiply_reduce_fusion.1), channel_id=1, replica_groups=mesh['gx'=64,'gy'=8] {'gx','gy'}, use_global_device_ids=true, to_apply=%region_11.12 | all-reduce | flops 128 | bytes 1024 | tf_op jit(solution)/shard_map/psum | solution.py:116
  973.8 99.7 %psum.47 = f32[128]{0:T(128)S(1)} all-reduce(f32[128]{0:T(128)S(1)} %multiply_reduce_fusion), channel_id=1, replica_groups=mesh['gx'=64,'gy'=8] {'gx','gy'}, use_global_device_ids=true, to_apply=%region_13.14 | all-reduce | flops 128 | bytes 1024 | tf_op jit(solution)/shard_map/psum | solution.py:112
  (78 shorter events, 22.4 us)
Async XLA Ops:
  0.6 202.7 %copy-start = (bf16[1,1,128,640]{3,2,1,0:T(8,128)(2,1)S(1)}, bf16[1,1,128,640]{3,2,1,0:T(8,128)(2,1)}, u32[]{:S(2)}) copy-start(bf16[1,1,128,640]{3,2,1,0:T(8,128)(2,1)} %param.12) | copy-start | bytes 491524
  116.1 14.2 %copy-start.5 = (s32[1,1,4,128]{3,2,1,0:T(4,128)S(1)}, s32[1,1,4,128]{3,2,1,0:T(4,128)}, u32[]{:S(2)}) copy-start(s32[1,1,4,128]{3,2,1,0:T(4,128)} %param.9) | copy-start | bytes 6148
  116.1 14.2 %copy-start.1 = (f32[1,1,128,128]{3,2,1,0:T(8,128)S(1)}, f32[1,1,128,128]{3,2,1,0:T(8,128)}, u32[]{:S(2)}) copy-start(f32[1,1,128,128]{3,2,1,0:T(8,128)} %param.8) | copy-start | bytes 196612
  116.1 25.8 %copy-start.7 = (s32[512]{0:T(512)S(1)}, s32[512]{0:T(512)}, u32[]{:S(2)}) copy-start(s32[512]{0:T(512)} %param.15) | copy-start | bytes 6148
  116.1 26.4 %copy-start.2 = (bf16[1,1,32,16384]{3,2,1,0:T(8,128)(2,1)S(1)}, bf16[1,1,32,16384]{3,2,1,0:T(8,128)(2,1)}, u32[]{:S(2)}) copy-start(bf16[1,1,32,16384]{3,2,1,0:T(8,128)(2,1)} %param.14) | copy-start | bytes 3145732
  116.1 201.9 %all-to-all-start = ((bf16[512,32,128]{2,1,0:T(8,128)(2,1)}), bf16[512,32,128]{2,1,0:T(8,128)(2,1)}, u32[]{:S(2)}, u32[]{:S(2)}) async-start(bf16[512,32,128]{2,1,0:T(8,128)(2,1)} %stack.13), calls=%async_computation | async-start | bytes 8388608 | tf_op jit(solution)/shard_map/all_to_all | solution.py:82
  131.7 71.6 %collective-permute-start = (bf16[1,128,128]{2,1,0:T(8,128)(2,1)S(1)}, bf16[1,128,128]{2,1,0:T(8,128)(2,1)S(1)}, u32[]{:S(2)}, u32[]{:S(2)}) collective-permute-start(bf16[1,128,128]{2,1,0:T(8,128)(2,1)S(1)} %get-tuple-element.23), channel_id=1, source_target_pairs={{0,8},{8,16},{16,24},{24,32},{32,40},{40,48},{48,56},{56,64},{64,7... | collective-permute-start | bytes 98312 | tf_op jit(solution)/shard_map/ppermute | solution.py:16
  135.0 68.3 %collective-permute-start.2 = (bf16[1,128,128]{2,1,0:T(8,128)(2,1)S(1)}, bf16[1,128,128]{2,1,0:T(8,128)(2,1)S(1)}, u32[]{:S(2)}, u32[]{:S(2)}) collective-permute-start(bf16[1,128,128]{2,1,0:T(8,128)(2,1)S(1)} %get-tuple-element.24), channel_id=1, source_target_pairs={{0,1},{1,2},{2,3},{3,4},{4,5},{5,6},{6,7},{8,9},{9,10},{10,11},{11... | collective-permute-start | bytes 98312 | tf_op jit(solution)/shard_map/ppermute | solution.py:16
  138.6 64.6 %collective-permute-start.1 = (bf16[1,128,128]{2,1,0:T(8,128)(2,1)S(1)}, bf16[1,128,128]{2,1,0:T(8,128)(2,1)S(1)}, u32[]{:S(2)}, u32[]{:S(2)}) collective-permute-start(bf16[1,128,128]{2,1,0:T(8,128)(2,1)S(1)} %get-tuple-element.25), channel_id=1, source_target_pairs={{8,0},{16,8},{24,16},{32,24},{40,32},{48,40},{56,48},{64,56},{72,6... | collective-permute-start | bytes 98312 | tf_op jit(solution)/shard_map/ppermute | solution.py:17
  139.9 63.3 %collective-permute-start.3 = (bf16[1,128,128]{2,1,0:T(8,128)(2,1)S(1)}, bf16[1,128,128]{2,1,0:T(8,128)(2,1)S(1)}, u32[]{:S(2)}, u32[]{:S(2)}) collective-permute-start(bf16[1,128,128]{2,1,0:T(8,128)(2,1)S(1)} %get-tuple-element.26), channel_id=1, source_target_pairs={{1,0},{2,1},{3,2},{4,3},{5,4},{6,5},{7,6},{9,8},{10,9},{11,10},{12... | collective-permute-start | bytes 98312 | tf_op jit(solution)/shard_map/ppermute | solution.py:17
  145.6 172.4 %copy-start.6 = (bf16[1,1,128,32]{2,3,1,0:T(8,128)(2,1)S(1)}, bf16[1,1,128,32]{2,3,1,0:T(8,128)(2,1)}, u32[]{:S(2)}) copy-start(bf16[1,1,128,32]{2,3,1,0:T(8,128)(2,1)} %param.13) | copy-start | bytes 24580
  318.0 22.1 %copy-start.4 = (f32[1,1,4,128]{3,2,1,0:T(4,128)S(1)}, f32[1,1,4,128]{3,2,1,0:T(4,128)}, u32[]{:S(2)}) copy-start(f32[1,1,4,128]{3,2,1,0:T(4,128)} %param.10) | copy-start | bytes 6148
  318.0 24.5 %copy-start.3 = (bf16[1,1,1,128,128]{4,3,2,1,0:T(8,128)(2,1)S(1)}, bf16[1,1,1,128,128]{4,3,2,1,0:T(8,128)(2,1)}, u32[]{:S(2)}) copy-start(bf16[1,1,1,128,128]{4,3,2,1,0:T(8,128)(2,1)} %param.11) | copy-start | bytes 98308
  326.6 10.2 collective-permute-start.4
  329.8 7.0 collective-permute-start.6
  333.6 5.2 collective-permute-start.5
  334.9 5.2 collective-permute-start.7
  546.8 201.0 %all-to-all-start.1 = ((bf16[512,32,128]{2,1,0:T(8,128)(2,1)}), bf16[512,32,128]{2,1,0:T(8,128)(2,1)}, u32[]{:S(2)}, u32[]{:S(2)}) async-start(bf16[512,32,128]{2,1,0:T(8,128)(2,1)} %stack.16), calls=%async_computation.1 | async-start | bytes 8388608 | tf_op jit(solution)/shard_map/all_to_all | solution.py:82
  561.4 10.2 collective-permute-start.8
  564.7 6.9 collective-permute-start.10
  568.3 5.2 collective-permute-start.9
  569.6 5.9 collective-permute-start.11
  756.4 10.2 collective-permute-start.12
  759.6 7.0 collective-permute-start.14
  763.3 5.2 collective-permute-start.13
  764.6 5.2 collective-permute-start.15
